TPU v7x, 256 devices: a whole 4x4x8 slice. The times are simulated.
256 devices in a mesh: ctx: 8 (over x, core), ch: 32 (over y, z).
Axes of the slice: x: 4, y: 4, z: 8, core: 2. Of those that a mesh axis runs over, the one named last changes fastest.
Arguments:
- tokens_in: bfloat16 [8192, 8192], P(('ctx', 'ch')), may hold values from -6 to 6
- norm_gain: float32 [8192], replicated, may hold values from 0.1 to 1.9
- proj_weight: bfloat16 [3, 8192, 8192], P(None, 'ctx', 'ch'), may hold values from -0.0625 to 0.0625
- conv_weight: float32 [3, 7, 8192], P(None, None, 'ch'), may hold values from -2 to 2
- decay_rate: float32 [16, 8192], P(None, 'ch'), may hold values from 6.1035157e-06 to 0.04
- residue: float32 [16, 8192], P(None, 'ch'), may hold values from -1.5 to 1.5
- skip_gain: float32 [8192], P('ch'), may hold values from -3 to 3
Outputs:
- gated: bfloat16 [8192, 8192], P(('ctx', 'ch'))
All inputs are finite; a program needn't handle non-finite values.
Results may differ from a plain program's by a relative error of at most 0.008.
Values may be sent and summed in bfloat16 or wider, within the bound.
No kernel may reach another device: no remote copies, remote signals or barrier semaphores. Data moves between devices by JAX's collectives and lax.ppermute only.
A program may use at most 128 MiB of HBM per device.

v0:
```python
import jax
import jax.numpy as jnp
from jax import lax
from jax.sharding import PartitionSpec as P

norm_eps = 1e-05


def shifted(shard, axis, by):
    length = lax.axis_size(axis)
    pairs = [(i, i + by) for i in range(length) if 0 <= i + by < length]
    return lax.ppermute(shard, axis, pairs)


def on_device(tokens_in, norm_gain, proj_weight, conv_weight, decay_rate, residue, skip_gain):
    widened = tokens_in.astype(jnp.float32)
    mean_square = jnp.mean(widened * widened, axis=-1, keepdims=True)
    normed = (widened * lax.rsqrt(mean_square + norm_eps) * norm_gain[None, :]).astype(jnp.bfloat16)
    gathered = lax.all_gather(normed, "ch", axis=0, tiled=True)
    row_count = gathered.shape[0]
    chan_count = proj_weight.shape[2]
    summed = jnp.einsum(
        "tf,ifc->itc",
        gathered,
        lax.all_gather(proj_weight, "ctx", axis=1, tiled=True),
        preferred_element_type=jnp.float32,
    )
    projected = summed.astype(jnp.bfloat16)
    tap_count = conv_weight.shape[1]
    reach = tap_count - 1
    rim_rows = shifted(projected[:, row_count - reach :, :], "ctx", 1)
    padded = jnp.concatenate([rim_rows, projected], axis=1).astype(jnp.float32)
    featured = jnp.zeros((3, row_count, chan_count), jnp.float32)
    for shift_idx in range(tap_count):
        featured = (
            featured
            + conv_weight[:, shift_idx, None, :]
            * padded[:, reach - shift_idx : reach - shift_idx + row_count, :]
        )
    queries = featured[0]
    mixed = featured[1] * featured[2]
    highest = lax.Precision.HIGHEST
    in_scale = jnp.sqrt(-jnp.expm1(-2.0 * decay_rate))
    span_rows = min(128, row_count)
    span_count = row_count // span_rows
    positions = jnp.arange(span_rows, dtype=jnp.float32)
    lag_decay = jnp.exp(-decay_rate[:, None, :] * positions[None, :, None])
    impulse = jnp.sum((residue * in_scale)[:, None, :] * lag_decay, axis=0)
    offsets = jnp.arange(span_rows)[:, None] - jnp.arange(span_rows)[None, :]
    lag_table = (offsets[None, :, :] == jnp.arange(span_rows)[:, None, None]).astype(jnp.float32)
    toeplitz = jnp.einsum("lc,lts->cts", impulse, lag_table, precision=highest)
    spans_in = mixed.reshape(span_count, span_rows, chan_count)
    inside = jnp.einsum("cts,jsc->jtc", toeplitz, spans_in, precision=highest)
    end_weight = in_scale[:, None, :] * jnp.exp(
        -decay_rate[:, None, :] * (span_rows - 1.0 - positions)[None, :, None]
    )
    span_ends = jnp.einsum("jsc,msc->jmc", spans_in, end_weight, precision=highest)
    span_decay = jnp.exp(-decay_rate * float(span_rows))

    def advance(carried, span_end):
        return (span_decay * carried + span_end, carried)

    zero_state = jnp.zeros(decay_rate.shape, jnp.float32)
    local_end, starts = lax.scan(advance, zero_state, span_ends)
    whole_decay = jnp.exp(-decay_rate * float(row_count))

    def handoff(unused_turn, incoming):
        return shifted(whole_decay * incoming + local_end, "ctx", 1)

    incoming = lax.fori_loop(0, lax.axis_size("ctx") - 1, handoff, zero_state)
    span_starts = jnp.arange(span_count, dtype=jnp.float32) * float(span_rows)
    starts = (
        starts
        + jnp.exp(-decay_rate[None, :, :] * span_starts[:, None, None]) * incoming[None, :, :]
    )
    out_weight = residue[:, None, :] * jnp.exp(
        -decay_rate[:, None, :] * (positions + 1.0)[None, :, None]
    )
    outside = jnp.einsum("jmc,mtc->jtc", starts, out_weight, precision=highest)
    filtered = (inside + outside).reshape(row_count, chan_count)
    gated = (queries * (filtered + skip_gain[None, :] * mixed)).astype(jnp.bfloat16)
    return lax.all_to_all(gated, "ch", split_axis=0, concat_axis=1, tiled=True)


def solution(mesh):
    in_specs = (
        P(("ctx", "ch"), None),
        P(),
        P(None, "ctx", "ch"),
        P(None, None, "ch"),
        P(None, "ch"),
        P(None, "ch"),
        P("ch"),
    )
    out_specs = P(("ctx", "ch"), None)
    return jax.shard_map(
        on_device, mesh=mesh, in_specs=in_specs, out_specs=out_specs, check_vma=False
    )
```

profile of v0, /device:TPU:34, one launch (start us, length us, event | category | flops | bytes accessed | tf_op | source)
XLA Modules:
  0.0 376.8 jit_solution(1986812862186608656)
XLA Ops:
  8.6 2.0 fusion.40
  10.9 1.7 multiply_reduce_fusion
  12.7 9.6 %fusion.4 = f32[256,128,128]{2,0,1:T(8,128)} fusion(s32[128,128]{1,0:T(8,128)S(1)} %iota_subtract_fusion, f32[128,256]{0,1:T(8,128)S(1)} %multiply_reduce_fusion), kind=kOutput, calls=%fused_computation.8 | convolution fusion | flops 6444548096 | bytes 16973824 | tf_op jit(solution)/shard_map/lc,lts->cts/dot_general | solution.py:51
  22.2 58.8 %all-gather.5.cloned.1.call-done = bf16[3,8192,256]{2,1,0:T(8,128)(2,1)} async-done(((bf16[3,1024,256]{2,1,0:T(8,128)(2,1)}), bf16[3,8192,256]{2,1,0:T(8,128)(2,1)}) %all-gather.5.cloned.1.call-update) | async-done | bytes 12582928 | tf_op jit(solution)/shard_map/all_gather | solution.py:25
  81.0 141.5 %all-gather.3.cloned.1.call-done = bf16[1024,8192]{1,0:T(8,128)(2,1)} async-done(((bf16[32,8192]{1,0:T(8,128)(2,1)}), bf16[1024,8192]{1,0:T(8,128)(2,1)}) %all-gather.3.cloned.1.call-update) | async-done | bytes 16777232 | tf_op jit(solution)/shard_map/all_gather | solution.py:19
  222.6 18.7 %fusion.23 = bf16[3,1024,256]{2,1,0:T(8,128)(2,1)S(1)} fusion(bf16[3,8192,256]{2,1,0:T(8,128)(2,1)} %all-gather.5.cloned.1.call-done, bf16[1024,8192]{1,0:T(8,128)(2,1)} %all-gather.3.cloned.1.call-done), kind=kOutput, calls=%fused_computation.34 | convolution fusion | flops 12885688320 | bytes 30932992 | tf_op jit(solution)/shard_map/tf,ifc->itc/dot_general | solution.py:22
  241.3 2.1 collective-permute-start.1
  244.3 2.0 collective-permute-done.1
  246.6 2.6 fusion.6
  249.8 38.4 %fusion.32 = f32[8,128,256]{1,0,2:T(8,128)} fusion(f32[8,128,256]{1,0,2:T(8,128)S(1)} %copy.29, f32[256,128,128]{2,0,1:T(8,128)} %fusion.4), kind=kOutput, calls=%fused_computation.37 | convolution fusion | flops 402653184 | bytes 18874368 | tf_op jit(solution)/shard_map/cts,jsc->jtc/dot_general | solution.py:53
  288.2 5.2 %fusion.29 = f32[8,16,256]{1,0,2:T(8,128)} fusion(f32[8,128,256]{1,0,2:T(8,128)S(1)} %copy.29, f32[128]{0:T(128)S(1)} %iota_subtract_fusion.1, f32[16,256]{0,1:T(8,128)S(1)} %copy.32, f32[16,256]{0,1:T(8,128)S(1)} %copy.28), kind=kOutput, calls=%fused_computation.36 | convolution fusion | flops 51380224 | bytes 1212928 | tf_op jit(solution)/shard_map/jsc,msc->jmc/dot_general | solution.py:57
  293.4 1.6 copy.34
  295.0 4.9 %while.24 = (s32[]{:T(128)}, f32[16,256]{1,0:T(8,128)S(1)}, f32[8,16,256]{2,1,0:T(8,128)}, f32[16,256]{1,0:T(8,128)S(1)}, f32[8,16,256]{2,1,0:T(8,128)S(1)}, /*index=5*/s32[]{:T(128)}, s32[]{:T(128)}) while((s32[]{:T(128)}, f32[16,256]{1,0:T(8,128)S(1)}, f32[8,16,256]{2,1,0:T(8,128)}, f32[16,256]{1,0:T(8,128)S(1)}, ...), condition=%wide.region_3.4_spmd.clone, body=%wide.region_2.3_spmd.clone.sunk | while | flops 16387 | bytes 98408 | solution.py:64
  299.9 35.4 %while.23 = (s32[]{:T(128)}, f32[16,256]{1,0:T(8,128)S(1)}, f32[16,256]{1,0:T(8,128)S(1)}, f32[16,256]{1,0:T(8,128)S(1)}, s32[]{:T(128)}) while((s32[]{:T(128)}, f32[16,256]{1,0:T(8,128)S(1)}, f32[16,256]{1,0:T(8,128)S(1)}, f32[16,256]{1,0:T(8,128)S(1)}, s32[]{:T(128)}) %tuple.55), condition=%wide.region_5.6_spmd, body=%wide.region_4.5_spmd.sunk | while | flops 8194 | bytes 131173 | solution.py:70
  299.9 1.9 collective-permute-start
  301.9 3.1 collective-permute-done
  305.0 1.9 collective-permute-start
  306.9 3.1 collective-permute-done
  310.1 1.9 collective-permute-start
  312.0 3.1 collective-permute-done
  315.1 1.9 collective-permute-start
  317.0 3.1 collective-permute-done
  320.2 1.9 collective-permute-start
  322.1 3.1 collective-permute-done
  325.2 1.9 collective-permute-start
  327.1 3.1 collective-permute-done
  330.3 1.9 collective-permute-start
  332.2 3.1 collective-permute-done
  336.3 1.3 copy.35
  337.7 5.0 %fusion.35 = f32[8,128,256]{1,0,2:T(8,128)} fusion(f32[8,128,256]{1,0,2:T(8,128)S(1)} %copy-done, f32[8,16,256]{1,0,2:T(8,128)} %copy.35, f32[128]{0:T(128)S(1)} %iota_add_fusion, f32[16,256]{0,1:T(8,128)} %copy.31, f32[16,256]{0,1:T(8,128)S(1)} %copy.28), kind=kOutput, calls=%fused_computation.38 | convolution fusion | flops 51642368 | bytes 2261504 | tf_op jit(solution)/shard_map/jmc,mtc->jtc/dot_general | solution.py:79
  342.6 1.6 copy.36
  344.6 24.5 %all_to_all.16 = bf16[32,32,256]{2,1,0:T(8,128)(2,1)S(1)} all-to-all(bf16[32,32,256]{2,1,0:T(8,128)(2,1)S(1)} %multiply_convert_fusion), channel_id=1, replica_groups=mesh['ctx'=8,'ch'=32] {'ch'}, dimensions={0} | all-to-all | bytes 1048576 | tf_op jit(solution)/shard_map/all_to_all | solution.py:82
  (63 shorter events, 11.3 us)
Async XLA Ops:
  6.5 4.1 %copy-start.3 = (f32[16,256]{1,0:T(8,128)S(1)}, f32[16,256]{1,0:T(8,128)}, u32[]{:S(2)}) copy-start(f32[16,256]{1,0:T(8,128)} %param.15) | copy-start | bytes 49156
  6.5 4.1 %copy-start.1 = (f32[16,256]{1,0:T(8,128)S(1)}, f32[16,256]{1,0:T(8,128)}, u32[]{:S(2)}) copy-start(f32[16,256]{1,0:T(8,128)} %param.16) | copy-start | bytes 49156
  6.5 6.1 %copy-start.2 = (f32[3,7,256]{2,1,0:T(8,128)S(1)}, f32[3,7,256]{2,1,0:T(8,128)}, u32[]{:S(2)}) copy-start(f32[3,7,256]{2,1,0:T(8,128)} %param.14) | copy-start | bytes 64516
  6.5 74.5 %all-gather.5.cloned.1.call-start = ((), (), s32[]{:S(2)}) async-start(), calls=%async_computation.2 | async-start | bytes 14155776 | tf_op jit(solution)/shard_map/all_gather | solution.py:25
  7.3 215.3 %all-gather.3.cloned.1.call-start = ((), (), s32[]{:S(2)}) async-start(), calls=%async_computation.1 | async-start | bytes 17301504 | tf_op jit(solution)/shard_map/all_gather | solution.py:19
  241.3 5.0 %collective-permute-start.1 = (bf16[3,6,256]{2,1,0:T(8,128)(2,1)S(1)}, bf16[3,6,256]{2,1,0:T(8,128)(2,1)S(1)}, u32[]{:S(2)}, u32[]{:S(2)}) collective-permute-start(bf16[3,6,256]{2,1,0:T(8,128)(2,1)S(1)} %slice.72), channel_id=1, source_target_pairs={{0,32},{32,64},{64,96},{96,128},{128,160},{160,192},{192,224},{1,3... | collective-permute-start | bytes 27656 | tf_op jit(solution)/shard_map/ppermute | solution.py:12
  293.4 44.3 %copy-start = (f32[8,128,256]{1,0,2:T(8,128)S(1)}, f32[8,128,256]{1,0,2:T(8,128)}, u32[]{:S(2)}) copy-start(f32[8,128,256]{1,0,2:T(8,128)} %fusion.32) | copy-start | bytes 3145732
  299.9 5.1 %collective-permute-start = (f32[16,256]{1,0:T(8,128)S(1)}, f32[16,256]{1,0:T(8,128)S(1)}, u32[]{:S(2)}, u32[]{:S(2)}) collective-permute-start(f32[16,256]{1,0:T(8,128)S(1)} %multiply_add_fusion.3), channel_id=1, source_target_pairs={{0,32},{32,64},{64,96},{96,128},{128,160},{160,192},{192,224},{1,3... | collective-permute-start | bytes 49160 | tf_op jit(solution)/shard_map/while/body/eval_jaxpr/ppermute | solution.py:12
  305.0 5.0 %collective-permute-start = (f32[16,256]{1,0:T(8,128)S(1)}, f32[16,256]{1,0:T(8,128)S(1)}, u32[]{:S(2)}, u32[]{:S(2)}) collective-permute-start(f32[16,256]{1,0:T(8,128)S(1)} %multiply_add_fusion.3), channel_id=1, source_target_pairs={{0,32},{32,64},{64,96},{96,128},{128,160},{160,192},{192,224},{1,3... | collective-permute-start | bytes 49160 | tf_op jit(solution)/shard_map/while/body/eval_jaxpr/ppermute | solution.py:12
  310.1 5.0 %collective-permute-start = (f32[16,256]{1,0:T(8,128)S(1)}, f32[16,256]{1,0:T(8,128)S(1)}, u32[]{:S(2)}, u32[]{:S(2)}) collective-permute-start(f32[16,256]{1,0:T(8,128)S(1)} %multiply_add_fusion.3), channel_id=1, source_target_pairs={{0,32},{32,64},{64,96},{96,128},{128,160},{160,192},{192,224},{1,3... | collective-permute-start | bytes 49160 | tf_op jit(solution)/shard_map/while/body/eval_jaxpr/ppermute | solution.py:12
  315.1 5.0 %collective-permute-start = (f32[16,256]{1,0:T(8,128)S(1)}, f32[16,256]{1,0:T(8,128)S(1)}, u32[]{:S(2)}, u32[]{:S(2)}) collective-permute-start(f32[16,256]{1,0:T(8,128)S(1)} %multiply_add_fusion.3), channel_id=1, source_target_pairs={{0,32},{32,64},{64,96},{96,128},{128,160},{160,192},{192,224},{1,3... | collective-permute-start | bytes 49160 | tf_op jit(solution)/shard_map/while/body/eval_jaxpr/ppermute | solution.py:12
  320.2 5.0 %collective-permute-start = (f32[16,256]{1,0:T(8,128)S(1)}, f32[16,256]{1,0:T(8,128)S(1)}, u32[]{:S(2)}, u32[]{:S(2)}) collective-permute-start(f32[16,256]{1,0:T(8,128)S(1)} %multiply_add_fusion.3), channel_id=1, source_target_pairs={{0,32},{32,64},{64,96},{96,128},{128,160},{160,192},{192,224},{1,3... | collective-permute-start | bytes 49160 | tf_op jit(solution)/shard_map/while/body/eval_jaxpr/ppermute | solution.py:12
  325.2 5.0 %collective-permute-start = (f32[16,256]{1,0:T(8,128)S(1)}, f32[16,256]{1,0:T(8,128)S(1)}, u32[]{:S(2)}, u32[]{:S(2)}) collective-permute-start(f32[16,256]{1,0:T(8,128)S(1)} %multiply_add_fusion.3), channel_id=1, source_target_pairs={{0,32},{32,64},{64,96},{96,128},{128,160},{160,192},{192,224},{1,3... | collective-permute-start | bytes 49160 | tf_op jit(solution)/shard_map/while/body/eval_jaxpr/ppermute | solution.py:12
  330.3 5.0 %collective-permute-start = (f32[16,256]{1,0:T(8,128)S(1)}, f32[16,256]{1,0:T(8,128)S(1)}, u32[]{:S(2)}, u32[]{:S(2)}) collective-permute-start(f32[16,256]{1,0:T(8,128)S(1)} %multiply_add_fusion.3), channel_id=1, source_target_pairs={{0,32},{32,64},{64,96},{96,128},{128,160},{160,192},{192,224},{1,3... | collective-permute-start | bytes 49160 | tf_op jit(solution)/shard_map/while/body/eval_jaxpr/ppermute | solution.py:12
  337.7 6.5 %copy-start.4 = (f32[256]{0:T(256)S(1)}, f32[256]{0:T(256)}, u32[]{:S(2)}) copy-start(f32[256]{0:T(256)} %param.17) | copy-start | bytes 3076
Sparse Core Ops, SparseCore 0:
  9.2 71.7 all-gather.4
  83.6 138.9 all-gather.2
where the time goes:
time: 377 us
  waiting for transfers between devices  225 us (60%)
  matrix products  76.7 us (20%)
  blocking collectives  24.5 us (6%)
  starting transfers between devices  15.5 us (4%)
  other arithmetic  14.5 us (4%)
  between operations  13.6 us (4%)
  local copies, waits for them, and re-layouts  6.84 us (2%)
    all_gather x1, waiting for transfers between devices, on_device(): gathered = lax.all_gather(normed, 'ch', axis=0, tiled=True)  142 us
    all_gather x1, waiting for transfers between devices, on_device(): lax.all_gather(proj_weight, 'ctx', axis=1, tiled=True)  58.8 us
    dot_general x1, matrix products, on_device(): inside = jnp.einsum('cts,jsc->jtc', toeplitz, spans_in, precision=highest)  38.4 us
    all_to_all x1, blocking collectives, on_device(): return lax.all_to_all(gated, 'ch', split_axis=0, concat_axis=1, tiled=True)  24.5 us
    ppermute x8, waiting for transfers between devices, shifted(): return lax.ppermute(shard, axis, pairs)  23.9 us
    dot_general x1, matrix products, on_device(): jnp.einsum('tf,ifc->itc', gathered, lax.all_gather(proj_weight, 'ctx', ax...  18.7 us
    ppermute x8, starting transfers between devices, shifted(): return lax.ppermute(shard, axis, pairs)  15.5 us
    dot_general x1, matrix products, on_device(): toeplitz = jnp.einsum('lc,lts->cts', impulse, lag_table, precision=highest)  9.55 us
  transfers between devices with their start and end apart: 10, of which 10 were waited for; matrix products, arithmetic and copies ran while one was open for 4% of the time, Pallas kernels for 0%

commit v1 on v0

--- a/solution.py
+++ b/solution.py
@@ -19,12 +19,38 @@
     gathered = lax.all_gather(normed, "ch", axis=0, tiled=True)
     row_count = gathered.shape[0]
     chan_count = proj_weight.shape[2]
-    summed = jnp.einsum(
+    size, index, rows = (lax.axis_size("ctx"), lax.axis_index("ctx"), proj_weight.shape[1])
+    ahead = [(i_2, (i_2 + 1) % size) for i_2 in range(size)]
+    left = [(i_2, (i_2 - 1) % size) for i_2 in range(size)]
+    half = size // 2
+    from_left = from_right = proj_weight
+    total = jnp.einsum(
         "tf,ifc->itc",
-        gathered,
-        lax.all_gather(proj_weight, "ctx", axis=1, tiled=True),
+        lax.dynamic_slice_in_dim(gathered, index * rows, proj_weight.shape[1], axis=1),
+        proj_weight,
         preferred_element_type=jnp.float32,
     )
+    for step in range(1, half + 1):
+        from_left = lax.ppermute(from_left, "ctx", ahead)
+        if step < size - half:
+            from_right = lax.ppermute(from_right, "ctx", left)
+            total = total + jnp.einsum(
+                "tf,ifc->itc",
+                lax.dynamic_slice_in_dim(
+                    gathered, (index + step) % size * rows, from_right.shape[1], axis=1
+                ),
+                from_right,
+                preferred_element_type=jnp.float32,
+            )
+        total = total + jnp.einsum(
+            "tf,ifc->itc",
+            lax.dynamic_slice_in_dim(
+                gathered, (index - step) % size * rows, from_left.shape[1], axis=1
+            ),
+            from_left,
+            preferred_element_type=jnp.float32,
+        )
+    summed = total
     projected = summed.astype(jnp.bfloat16)
     tap_count = conv_weight.shape[1]
     reach = tap_count - 1

time: 377 us -> 313 us (0.83)
  waiting for transfers between devices: 225 us -> 147 us
  matrix products: 76.7 us -> 83.8 us
  starting transfers between devices: 15.5 us -> 20.4 us
    all_gather x1, waiting for transfers between devices: 142 us -> 80.5 us  [on_device(): gathered = lax.all_gather(normed, 'ch', axis=0, tiled=True)]
    all_gather x1 -> x0, waiting for transfers between devices: 58.8 us -> none  [on_device(): lax.all_gather(proj_weight, 'ctx', axis=1, tiled=True)]
    ppermute x0 -> x7, waiting for transfers between devices: none -> 42.6 us  [the longest x4 42.6 us: on_device(): from_left = lax.ppermute(from_left, 'ctx', ahead)]
    dot_general x1 -> x8, matrix products: 18.7 us -> 27.5 us  [the longest x4 15.6 us: on_device(): jnp.einsum('tf,ifc->itc', lax.dynamic_slice_in_dim(gathered, (index - ste...]
    ppermute x0 -> x7, starting transfers between devices: none -> 5.06 us  [the longest x3 5.03 us: on_device(): from_right = lax.ppermute(from_right, 'ctx', left)]
  transfers between devices with their start and end apart: 10 -> 16, of which waited for: 10 -> 12; matrix products, arithmetic and copies ran while one was open for 4% -> 11% of each run, Pallas kernels for 0% -> 0%
where the time goes in v1:
time: 313 us; the launch traced here: 312 us
  waiting for transfers between devices  147 us (47%)
  matrix products  83.8 us (27%)
  blocking collectives  24.5 us (8%)
  starting transfers between devices  20.4 us (7%)
  other arithmetic  15.5 us (5%)
  between operations  13.8 us (4%)
  local copies, waits for them, and re-layouts  6.79 us (2%)
    all_gather x1, waiting for transfers between devices, on_device(): gathered = lax.all_gather(normed, 'ch', axis=0, tiled=True)  80.5 us
    ppermute x4, waiting for transfers between devices, on_device(): from_left = lax.ppermute(from_left, 'ctx', ahead)  42.6 us
    dot_general x1, matrix products, on_device(): inside = jnp.einsum('cts,jsc->jtc', toeplitz, spans_in, precision=highest)  37.7 us
    all_to_all x1, blocking collectives, on_device(): return lax.all_to_all(gated, 'ch', split_axis=0, concat_axis=1, tiled=True)  24.5 us
    ppermute x8, waiting for transfers between devices, shifted(): return lax.ppermute(shard, axis, pairs)  24.1 us
    dot_general x4, matrix products, on_device(): jnp.einsum('tf,ifc->itc', lax.dynamic_slice_in_dim(gathered, (index - ste...  15.6 us
    ppermute x8, starting transfers between devices, shifted(): return lax.ppermute(shard, axis, pairs)  15.3 us
    dot_general x3, matrix products, on_device(): jnp.einsum('tf,ifc->itc', lax.dynamic_slice_in_dim(gathered, (index + ste...  10.1 us
  transfers between devices with their start and end apart: 16, of which 12 were waited for; matrix products, arithmetic and copies ran while one was open for 11% of the time, Pallas kernels for 0%

profile of v1, /device:TPU:34, one launch (start us, length us, event | category | flops | bytes accessed | tf_op | source)
XLA Modules:
  0.0 312.0 jit_solution(15841955197676510585)
XLA Ops:
  7.8 2.0 fusion.59
  11.6 18.3 %collective-permute-done.2 = bf16[3,1024,256]{2,1,0:T(8,128)(2,1)S(1)} collective-permute-done((bf16[3,1024,256]{2,1,0:T(8,128)(2,1)}, bf16[3,1024,256]{2,1,0:T(8,128)(2,1)S(1)}, u32[]{:S(2)}, u32[]{:S(2)}) %collective-permute-start.2) | collective-permute-done | bytes 1572896 | tf_op jit(solution)/shard_map/ppermute | solution.py:34
  34.4 15.5 %collective-permute-done.4 = bf16[3,1024,256]{2,1,0:T(8,128)(2,1)} collective-permute-done((bf16[3,1024,256]{2,1,0:T(8,128)(2,1)S(1)}, bf16[3,1024,256]{2,1,0:T(8,128)(2,1)}, u32[]{:S(2)}, u32[]{:S(2)}) %collective-permute-start.4) | collective-permute-done | bytes 1572896 | tf_op jit(solution)/shard_map/ppermute | solution.py:34
  50.1 9.5 %fusion.2 = f32[256,128,128]{2,0,1:T(8,128)} fusion(s32[128,128]{1,0:T(8,128)S(1)} %iota_subtract_fusion, f32[128,256]{0,1:T(8,128)S(1)} %multiply_reduce_fusion), kind=kOutput, calls=%fused_computation.6 | convolution fusion | flops 6444548096 | bytes 16973824 | tf_op jit(solution)/shard_map/lc,lts->cts/dot_general | solution.py:77
  61.2 8.8 %collective-permute-done.6 = bf16[3,1024,256]{2,1,0:T(8,128)(2,1)} collective-permute-done((bf16[3,1024,256]{2,1,0:T(8,128)(2,1)}, bf16[3,1024,256]{2,1,0:T(8,128)(2,1)}, u32[]{:S(2)}, u32[]{:S(2)}) %collective-permute-start.6) | collective-permute-done | bytes 1572896 | tf_op jit(solution)/shard_map/ppermute | solution.py:34
  70.0 80.5 %all-gather.2.cloned.1.call-done = bf16[1024,8192]{1,0:T(8,128)(2,1)} async-done(((bf16[32,8192]{1,0:T(8,128)(2,1)}), bf16[1024,8192]{1,0:T(8,128)(2,1)}) %all-gather.2.cloned.1.call-update) | async-done | bytes 16777232 | tf_op jit(solution)/shard_map/all_gather | solution.py:19
  150.5 4.0 %fusion.12 = f32[1024,3,256]{2,0,1:T(8,128)S(1)} fusion(bf16[3,1024,256]{2,1,0:T(8,128)(2,1)} %collective-permute-done.6, bf16[1024,8192]{1,0:T(8,128)(2,1)} %all-gather.2.cloned.1.call-done, s32[]{:T(128)S(6)} %select_n.67), kind=kOutput, calls=%fused_computation.24 | convolution fusion | flops 1610612736 | bytes 6815748 | tf_op jit(solution)/shard_map/tf,ifc->itc/dot_general | solution.py:45
  154.5 4.6 %fusion.16 = f32[1024,3,256]{2,0,1:T(8,128)S(1)} fusion(bf16[3,1024,256]{2,1,0:T(8,128)(2,1)} %collective-permute-done.4, bf16[1024,8192]{1,0:T(8,128)(2,1)} %all-gather.2.cloned.1.call-done, s32[]{:T(128)S(6)} %select_n.63), kind=kOutput, calls=%fused_computation.28 | convolution fusion | flops 1610612736 | bytes 6815748 | tf_op jit(solution)/shard_map/tf,ifc->itc/dot_general | solution.py:45
  159.1 3.3 %fusion.18 = f32[1024,3,256]{2,0,1:T(8,128)S(1)} fusion(bf16[3,1024,256]{2,1,0:T(8,128)(2,1)} %collective-permute-done.3, bf16[1024,8192]{1,0:T(8,128)(2,1)S(1)} %copy-done.1, s32[]{:T(128)S(6)} %select_n.61), kind=kOutput, calls=%fused_computation.30 | convolution fusion | flops 1610612736 | bytes 6815748 | tf_op jit(solution)/shard_map/tf,ifc->itc/dot_general | solution.py:37
  164.3 3.3 %fusion.22 = f32[1024,3,256]{2,0,1:T(8,128)S(1)} fusion(bf16[3,1024,256]{2,1,0:T(8,128)(2,1)} %collective-permute-done.1, bf16[1024,8192]{1,0:T(8,128)(2,1)S(1)} %copy-done.1, s32[]{:T(128)S(6)} %select_n.57), kind=kOutput, calls=%fused_computation.34 | convolution fusion | flops 1610612736 | bytes 6815748 | tf_op jit(solution)/shard_map/tf,ifc->itc/dot_general | solution.py:37
  169.5 3.4 %fusion.14 = f32[1024,3,256]{2,0,1:T(8,128)} fusion(bf16[3,1024,256]{2,1,0:T(8,128)(2,1)S(1)} %collective-permute-done.5, bf16[1024,8192]{1,0:T(8,128)(2,1)S(1)} %copy-done.1, s32[]{:T(128)S(6)} %select_n.65), kind=kOutput, calls=%fused_computation.26 | convolution fusion | flops 1610612736 | bytes 6815748 | tf_op jit(solution)/shard_map/tf,ifc->itc/dot_general | solution.py:37
  172.9 5.2 %fusion.42 = bf16[3,1024,256]{2,1,0:T(8,128)(2,1)S(1)} fusion(f32[1024,3,256]{2,0,1:T(8,128)S(1)} %fusion.12, f32[1024,3,256]{2,0,1:T(8,128)} %fusion.14, f32[1024,3,256]{2,0,1:T(8,128)S(1)} %fusion.16, f32[1024,3,256]{2,0,1:T(8,128)S(1)} %fusion.18, f32[1024,3,256]{2,0,1:T(8,128)S(1)} %fusion.20, f32[1024,3,256]{2,0,1:T(8,128)S(1)} %fusion.24, ...), kind=kOutput, calls=%fused_computation.56 | convolution fusion | flops 1616904192 | bytes 27262980 | tf_op jit(solution)/shard_map/tf,ifc->itc/dot_general | solution.py:45
  178.2 1.9 collective-permute-start.8
  181.0 2.2 collective-permute-done.8
  183.5 2.8 fusion.4
  186.9 5.2 %fusion.46 = f32[8,16,256]{1,0,2:T(8,128)} fusion(f32[8,128,256]{1,0,2:T(8,128)S(1)} %copy.29, f32[128]{0:T(128)S(1)} %iota_subtract_fusion.1, f32[16,256]{0,1:T(8,128)S(1)} %copy.32, f32[16,256]{0,1:T(8,128)S(1)} %copy.28), kind=kOutput, calls=%fused_computation.58 | convolution fusion | flops 51380224 | bytes 1212928 | tf_op jit(solution)/shard_map/jsc,msc->jmc/dot_general | solution.py:83
  193.6 4.9 %while.24 = (s32[]{:T(128)}, f32[16,256]{1,0:T(8,128)S(1)}, f32[8,16,256]{2,1,0:T(8,128)}, f32[16,256]{1,0:T(8,128)S(1)}, f32[8,16,256]{2,1,0:T(8,128)S(1)}, /*index=5*/s32[]{:T(128)}, s32[]{:T(128)}) while((s32[]{:T(128)}, f32[16,256]{1,0:T(8,128)S(1)}, f32[8,16,256]{2,1,0:T(8,128)}, f32[16,256]{1,0:T(8,128)S(1)}, ...), condition=%wide.region_3.4_spmd.clone, body=%wide.region_2.3_spmd.clone.sunk | while | flops 16387 | bytes 98908 | solution.py:90
  198.6 35.4 %while.23 = (s32[]{:T(128)}, f32[16,256]{1,0:T(8,128)S(1)}, f32[16,256]{1,0:T(8,128)S(1)}, f32[16,256]{1,0:T(8,128)S(1)}, s32[]{:T(128)}) while((s32[]{:T(128)}, f32[16,256]{1,0:T(8,128)S(1)}, f32[16,256]{1,0:T(8,128)S(1)}, f32[16,256]{1,0:T(8,128)S(1)}, s32[]{:T(128)}) %tuple.55), condition=%wide.region_5.6_spmd, body=%wide.region_4.5_spmd.sunk | while | flops 8194 | bytes 131173 | solution.py:96
  198.6 1.9 collective-permute-start
  200.5 3.1 %collective-permute-done = f32[16,256]{1,0:T(8,128)S(1)} collective-permute-done((f32[16,256]{1,0:T(8,128)S(1)}, f32[16,256]{1,0:T(8,128)S(1)}, u32[]{:S(2)}, u32[]{:S(2)}) %collective-permute-start) | collective-permute-done | bytes 16416 | tf_op jit(solution)/shard_map/while/body/eval_jaxpr/ppermute | solution.py:12
  203.7 1.9 collective-permute-start
  205.6 3.1 %collective-permute-done = f32[16,256]{1,0:T(8,128)S(1)} collective-permute-done((f32[16,256]{1,0:T(8,128)S(1)}, f32[16,256]{1,0:T(8,128)S(1)}, u32[]{:S(2)}, u32[]{:S(2)}) %collective-permute-start) | collective-permute-done | bytes 16416 | tf_op jit(solution)/shard_map/while/body/eval_jaxpr/ppermute | solution.py:12
  208.7 1.9 collective-permute-start
  210.6 3.1 %collective-permute-done = f32[16,256]{1,0:T(8,128)S(1)} collective-permute-done((f32[16,256]{1,0:T(8,128)S(1)}, f32[16,256]{1,0:T(8,128)S(1)}, u32[]{:S(2)}, u32[]{:S(2)}) %collective-permute-start) | collective-permute-done | bytes 16416 | tf_op jit(solution)/shard_map/while/body/eval_jaxpr/ppermute | solution.py:12
  213.8 1.9 collective-permute-start
  215.7 3.1 %collective-permute-done = f32[16,256]{1,0:T(8,128)S(1)} collective-permute-done((f32[16,256]{1,0:T(8,128)S(1)}, f32[16,256]{1,0:T(8,128)S(1)}, u32[]{:S(2)}, u32[]{:S(2)}) %collective-permute-start) | collective-permute-done | bytes 16416 | tf_op jit(solution)/shard_map/while/body/eval_jaxpr/ppermute | solution.py:12
  220.8 3.1 %collective-permute-done = f32[16,256]{1,0:T(8,128)S(1)} collective-permute-done((f32[16,256]{1,0:T(8,128)S(1)}, f32[16,256]{1,0:T(8,128)S(1)}, u32[]{:S(2)}, u32[]{:S(2)}) %collective-permute-start) | collective-permute-done | bytes 16416 | tf_op jit(solution)/shard_map/while/body/eval_jaxpr/ppermute | solution.py:12
  225.8 3.1 %collective-permute-done = f32[16,256]{1,0:T(8,128)S(1)} collective-permute-done((f32[16,256]{1,0:T(8,128)S(1)}, f32[16,256]{1,0:T(8,128)S(1)}, u32[]{:S(2)}, u32[]{:S(2)}) %collective-permute-start) | collective-permute-done | bytes 16416 | tf_op jit(solution)/shard_map/while/body/eval_jaxpr/ppermute | solution.py:12
  230.9 3.1 %collective-permute-done = f32[16,256]{1,0:T(8,128)S(1)} collective-permute-done((f32[16,256]{1,0:T(8,128)S(1)}, f32[16,256]{1,0:T(8,128)S(1)}, u32[]{:S(2)}, u32[]{:S(2)}) %collective-permute-start) | collective-permute-done | bytes 16416 | tf_op jit(solution)/shard_map/while/body/eval_jaxpr/ppermute | solution.py:12
  236.3 37.7 %fusion.49 = f32[8,128,256]{1,0,2:T(8,128)S(1)} fusion(f32[8,128,256]{1,0,2:T(8,128)S(1)} %copy.29, f32[256,128,128]{2,0,1:T(8,128)} %fusion.2), kind=kOutput, calls=%fused_computation.59 | convolution fusion | flops 402653184 | bytes 18874368 | tf_op jit(solution)/shard_map/cts,jsc->jtc/dot_general | solution.py:79
  274.1 3.9 %fusion.52 = f32[8,128,256]{1,0,2:T(8,128)} fusion(f32[8,128,256]{1,0,2:T(8,128)S(1)} %fusion.49, f32[8,16,256]{1,0,2:T(8,128)S(1)} %copy-done, f32[128]{0:T(128)S(1)} %iota_add_fusion, f32[16,256]{0,1:T(8,128)S(1)} %copy-done.2, f32[16,256]{0,1:T(8,128)S(1)} %copy.28), kind=kOutput, calls=%fused_computation.60 | convolution fusion | flops 51642368 | bytes 2261504 | tf_op jit(solution)/shard_map/jmc,mtc->jtc/dot_general | solution.py:105
  279.9 24.5 %all_to_all.16 = bf16[32,32,256]{2,1,0:T(8,128)(2,1)S(1)} all-to-all(bf16[32,32,256]{2,1,0:T(8,128)(2,1)S(1)} %multiply_convert_fusion), channel_id=1, replica_groups=mesh['ctx'=8,'ch'=32] {'ch'}, dimensions={0} | all-to-all | bytes 1048576 | tf_op jit(solution)/shard_map/all_to_all | solution.py:108
  (89 shorter events, 31.8 us)
Async XLA Ops:
  6.5 43.5 %copy-start.4 = (f32[3,7,256]{2,1,0:T(8,128)S(1)}, f32[3,7,256]{2,1,0:T(8,128)}, u32[]{:S(2)}) copy-start(f32[3,7,256]{2,1,0:T(8,128)} %param.14) | copy-start | bytes 64516
  6.5 144.0 %all-gather.2.cloned.1.call-start = ((), (), s32[]{:S(2)}) async-start(), calls=%async_computation.1 | async-start | bytes 17301504 | tf_op jit(solution)/shard_map/all_gather | solution.py:19
  9.9 20.1 %collective-permute-start.2 = (bf16[3,1024,256]{2,1,0:T(8,128)(2,1)}, bf16[3,1024,256]{2,1,0:T(8,128)(2,1)S(1)}, u32[]{:S(2)}, u32[]{:S(2)}) collective-permute-start(bf16[3,1024,256]{2,1,0:T(8,128)(2,1)} %param.13), channel_id=1, source_target_pairs={{0,32},{32,64},{64,96},{96,128},{128,160},{160,192},{192,224},{224... | collective-permute-start | bytes 4718600 | tf_op jit(solution)/shard_map/ppermute | solution.py:34
  9.9 22.8 %collective-permute-start.1 = (bf16[3,1024,256]{2,1,0:T(8,128)(2,1)}, bf16[3,1024,256]{2,1,0:T(8,128)(2,1)}, u32[]{:S(2)}, u32[]{:S(2)}) collective-permute-start(bf16[3,1024,256]{2,1,0:T(8,128)(2,1)} %param.13), channel_id=1, source_target_pairs={{0,224},{32,0},{64,32},{96,64},{128,96},{160,128},{192,160},{224,1... | collective-permute-start | bytes 4718600 | tf_op jit(solution)/shard_map/ppermute | solution.py:36
  29.9 29.7 %copy-start.7 = (bf16[3,1024,256]{2,1,0:T(8,128)(2,1)}, bf16[3,1024,256]{2,1,0:T(8,128)(2,1)S(1)}, u32[]{:S(2)}) copy-start(bf16[3,1024,256]{2,1,0:T(8,128)(2,1)S(1)} %collective-permute-done.2) | copy-start | bytes 4718596
  29.9 19.9 %collective-permute-start.4 = (bf16[3,1024,256]{2,1,0:T(8,128)(2,1)S(1)}, bf16[3,1024,256]{2,1,0:T(8,128)(2,1)}, u32[]{:S(2)}, u32[]{:S(2)}) collective-permute-start(bf16[3,1024,256]{2,1,0:T(8,128)(2,1)S(1)} %collective-permute-done.2), channel_id=1, source_target_pairs={{0,32},{32,64},{64,96},{96,128},{128,160},{160,192},{192,224},{224... | collective-permute-start | bytes 4718600 | tf_op jit(solution)/shard_map/ppermute | solution.py:34
  32.7 27.0 %collective-permute-start.3 = (bf16[3,1024,256]{2,1,0:T(8,128)(2,1)}, bf16[3,1024,256]{2,1,0:T(8,128)(2,1)}, u32[]{:S(2)}, u32[]{:S(2)}) collective-permute-start(bf16[3,1024,256]{2,1,0:T(8,128)(2,1)} %collective-permute-done.1), channel_id=1, source_target_pairs={{0,224},{32,0},{64,32},{96,64},{128,96},{160,128},{192,160},{224,1... | collective-permute-start | bytes 4718600 | tf_op jit(solution)/shard_map/ppermute | solution.py:36
  49.9 20.2 %collective-permute-start.6 = (bf16[3,1024,256]{2,1,0:T(8,128)(2,1)}, bf16[3,1024,256]{2,1,0:T(8,128)(2,1)}, u32[]{:S(2)}, u32[]{:S(2)}) collective-permute-start(bf16[3,1024,256]{2,1,0:T(8,128)(2,1)} %collective-permute-done.4), channel_id=1, source_target_pairs={{0,32},{32,64},{64,96},{96,128},{128,160},{160,192},{192,224},{224... | collective-permute-start | bytes 4718600 | tf_op jit(solution)/shard_map/ppermute | solution.py:34
  59.7 109.8 %collective-permute-start.5 = (bf16[3,1024,256]{2,1,0:T(8,128)(2,1)}, bf16[3,1024,256]{2,1,0:T(8,128)(2,1)S(1)}, u32[]{:S(2)}, u32[]{:S(2)}) collective-permute-start(bf16[3,1024,256]{2,1,0:T(8,128)(2,1)} %collective-permute-done.3), channel_id=1, source_target_pairs={{0,224},{32,0},{64,32},{96,64},{128,96},{160,128},{192,160},{224,1... | collective-permute-start | bytes 4718600 | tf_op jit(solution)/shard_map/ppermute | solution.py:36
  70.0 102.9 %collective-permute-start.7 = (bf16[3,1024,256]{2,1,0:T(8,128)(2,1)}, bf16[3,1024,256]{2,1,0:T(8,128)(2,1)S(1)}, u32[]{:S(2)}, u32[]{:S(2)}) collective-permute-start(bf16[3,1024,256]{2,1,0:T(8,128)(2,1)} %collective-permute-done.6), channel_id=1, source_target_pairs={{0,32},{32,64},{64,96},{96,128},{128,160},{160,192},{192,224},{224... | collective-permute-start | bytes 4718600 | tf_op jit(solution)/shard_map/ppermute | solution.py:34
  150.5 8.6 %copy-start.1 = (bf16[1024,8192]{1,0:T(8,128)(2,1)S(1)}, bf16[1024,8192]{1,0:T(8,128)(2,1)}, u32[]{:S(2)}) copy-start(bf16[1024,8192]{1,0:T(8,128)(2,1)} %all-gather.2.cloned.1.call-done) | copy-start | bytes 50331652
  159.1 3.3 %copy-start.8 = (bf16[3,1024,256]{2,1,0:T(8,128)(2,1)S(1)}, bf16[3,1024,256]{2,1,0:T(8,128)(2,1)}, u32[]{:S(2)}) copy-start(bf16[3,1024,256]{2,1,0:T(8,128)(2,1)} %copy-done.7) | copy-start | bytes 4718596
  164.3 3.3 %copy-start.6 = (bf16[3,1024,256]{2,1,0:T(8,128)(2,1)S(1)}, bf16[3,1024,256]{2,1,0:T(8,128)(2,1)}, u32[]{:S(2)}) copy-start(bf16[3,1024,256]{2,1,0:T(8,128)(2,1)} %param.13) | copy-start | bytes 4718596
  172.9 7.2 %copy-start.3 = (f32[16,256]{1,0:T(8,128)S(1)}, f32[16,256]{1,0:T(8,128)}, u32[]{:S(2)}) copy-start(f32[16,256]{1,0:T(8,128)} %param.16) | copy-start | bytes 49156
  178.2 5.0 %collective-permute-start.8 = (bf16[3,6,256]{2,1,0:T(8,128)(2,1)S(1)}, bf16[3,6,256]{2,1,0:T(8,128)(2,1)S(1)}, u32[]{:S(2)}, u32[]{:S(2)}) collective-permute-start(bf16[3,6,256]{2,1,0:T(8,128)(2,1)S(1)} %slice.72), channel_id=1, source_target_pairs={{0,32},{32,64},{64,96},{96,128},{128,160},{160,192},{192,224},{1,3... | collective-permute-start | bytes 27656 | tf_op jit(solution)/shard_map/ppermute | solution.py:12
  198.6 5.1 %collective-permute-start = (f32[16,256]{1,0:T(8,128)S(1)}, f32[16,256]{1,0:T(8,128)S(1)}, u32[]{:S(2)}, u32[]{:S(2)}) collective-permute-start(f32[16,256]{1,0:T(8,128)S(1)} %multiply_add_fusion.3), channel_id=1, source_target_pairs={{0,32},{32,64},{64,96},{96,128},{128,160},{160,192},{192,224},{1,3... | collective-permute-start | bytes 49160 | tf_op jit(solution)/shard_map/while/body/eval_jaxpr/ppermute | solution.py:12
  203.7 5.0 %collective-permute-start = (f32[16,256]{1,0:T(8,128)S(1)}, f32[16,256]{1,0:T(8,128)S(1)}, u32[]{:S(2)}, u32[]{:S(2)}) collective-permute-start(f32[16,256]{1,0:T(8,128)S(1)} %multiply_add_fusion.3), channel_id=1, source_target_pairs={{0,32},{32,64},{64,96},{96,128},{128,160},{160,192},{192,224},{1,3... | collective-permute-start | bytes 49160 | tf_op jit(solution)/shard_map/while/body/eval_jaxpr/ppermute | solution.py:12
  208.7 5.0 %collective-permute-start = (f32[16,256]{1,0:T(8,128)S(1)}, f32[16,256]{1,0:T(8,128)S(1)}, u32[]{:S(2)}, u32[]{:S(2)}) collective-permute-start(f32[16,256]{1,0:T(8,128)S(1)} %multiply_add_fusion.3), channel_id=1, source_target_pairs={{0,32},{32,64},{64,96},{96,128},{128,160},{160,192},{192,224},{1,3... | collective-permute-start | bytes 49160 | tf_op jit(solution)/shard_map/while/body/eval_jaxpr/ppermute | solution.py:12
  213.8 5.0 %collective-permute-start = (f32[16,256]{1,0:T(8,128)S(1)}, f32[16,256]{1,0:T(8,128)S(1)}, u32[]{:S(2)}, u32[]{:S(2)}) collective-permute-start(f32[16,256]{1,0:T(8,128)S(1)} %multiply_add_fusion.3), channel_id=1, source_target_pairs={{0,32},{32,64},{64,96},{96,128},{128,160},{160,192},{192,224},{1,3... | collective-permute-start | bytes 49160 | tf_op jit(solution)/shard_map/while/body/eval_jaxpr/ppermute | solution.py:12
  218.8 5.0 %collective-permute-start = (f32[16,256]{1,0:T(8,128)S(1)}, f32[16,256]{1,0:T(8,128)S(1)}, u32[]{:S(2)}, u32[]{:S(2)}) collective-permute-start(f32[16,256]{1,0:T(8,128)S(1)} %multiply_add_fusion.3), channel_id=1, source_target_pairs={{0,32},{32,64},{64,96},{96,128},{128,160},{160,192},{192,224},{1,3... | collective-permute-start | bytes 49160 | tf_op jit(solution)/shard_map/while/body/eval_jaxpr/ppermute | solution.py:12
  223.9 5.0 %collective-permute-start = (f32[16,256]{1,0:T(8,128)S(1)}, f32[16,256]{1,0:T(8,128)S(1)}, u32[]{:S(2)}, u32[]{:S(2)}) collective-permute-start(f32[16,256]{1,0:T(8,128)S(1)} %multiply_add_fusion.3), channel_id=1, source_target_pairs={{0,32},{32,64},{64,96},{96,128},{128,160},{160,192},{192,224},{1,3... | collective-permute-start | bytes 49160 | tf_op jit(solution)/shard_map/while/body/eval_jaxpr/ppermute | solution.py:12
  228.9 5.0 %collective-permute-start = (f32[16,256]{1,0:T(8,128)S(1)}, f32[16,256]{1,0:T(8,128)S(1)}, u32[]{:S(2)}, u32[]{:S(2)}) collective-permute-start(f32[16,256]{1,0:T(8,128)S(1)} %multiply_add_fusion.3), channel_id=1, source_target_pairs={{0,32},{32,64},{64,96},{96,128},{128,160},{160,192},{192,224},{1,3... | collective-permute-start | bytes 49160 | tf_op jit(solution)/shard_map/while/body/eval_jaxpr/ppermute | solution.py:12
  236.3 37.7 %copy-start = (f32[8,16,256]{1,0,2:T(8,128)S(1)}, f32[8,16,256]{1,0,2:T(8,128)}, u32[]{:S(2)}) copy-start(f32[8,16,256]{1,0,2:T(8,128)} %copy.35) | copy-start | bytes 393220
  236.3 37.7 %copy-start.2 = (f32[16,256]{0,1:T(8,128)S(1)}, f32[16,256]{0,1:T(8,128)}, u32[]{:S(2)}) copy-start(f32[16,256]{0,1:T(8,128)} %copy.31) | copy-start | bytes 49156
  274.0 5.4 %copy-start.5 = (f32[256]{0:T(256)S(1)}, f32[256]{0:T(256)}, u32[]{:S(2)}) copy-start(f32[256]{0:T(256)} %param.17) | copy-start | bytes 3076
Sparse Core Ops, SparseCore 0:
  10.0 140.4 all-gather.1
